TPU v7x, 32 devices: a whole 2x2x4 slice. The times are simulated.
32 devices in a mesh: dp: 4 (over x, core), tensor: 8 (over z, y).
Axes of the slice: x: 2, y: 2, z: 4, core: 2. Of those that a mesh axis runs over, the one named last changes fastest.
Arguments:
- grad: bfloat16 [4, 576, 6144], P('dp', 'tensor'), as said below
- momentum: float32 [4, 576, 6144], P('dp', 'tensor'), may hold values from -6 to 6
- owner: int32 [4], replicated, may hold values from 0 to 3, each once
Outputs:
- update: bfloat16 [4, 576, 6144], P(None, 'tensor')
- new_momentum: float32 [4, 576, 6144], P('dp', 'tensor')
Inputs may be any that keep to these rules, and one draw needn't show every extreme that they name: owner names each matrix 0 to 3 exactly once. `grad`: gradient entries are finite; every matrix has full rank.
All inputs are finite; a program needn't handle non-finite values.
Results may differ from a plain program's by a relative error of at most 0.0013.
The roundings to bfloat16 on the way count: a program that leaves them out, or rounds other values in their place, can miss the bound.
Values may be sent and summed in bfloat16 or wider, within the bound.
No kernel may reach another device: no remote copies, remote signals or barrier semaphores. Data moves between devices by JAX's collectives and lax.ppermute only.
A program may use at most 64 MiB of HBM per device.

v0:
```python
import math
import jax
import jax.numpy as jnp
from jax import lax
from jax.sharding import PartitionSpec as P

M = 576
N = 6144
ITERS = 2
coef_a = 3.4445
coef_b = -4.775
coef_c = 2.0315
decay = 0.95
eps = 1e-07


def per_device(grad, momentum, owner):
    new_momentum = decay * momentum + grad.astype(jnp.float32)
    direction = grad.astype(jnp.float32) + decay * new_momentum
    total = lax.psum(jnp.sum(direction * direction), "tensor")
    rows_here = (direction[0] / (jnp.sqrt(total) + eps)).astype(jnp.bfloat16)
    columns = lax.all_to_all(rows_here, "tensor", split_axis=1, concat_axis=0, tiled=True)
    for step in range(ITERS):
        gram = lax.psum(
            jnp.dot(columns, columns.T, preferred_element_type=jnp.float32), "tensor"
        ).astype(jnp.bfloat16)
        square = jnp.dot(gram, gram, preferred_element_type=jnp.float32)
        poly = (coef_b * gram.astype(jnp.float32) + coef_c * square).astype(jnp.bfloat16)
        applied = jnp.dot(poly, columns, preferred_element_type=jnp.float32)
        columns = (coef_a * columns.astype(jnp.float32) + applied).astype(jnp.bfloat16)
    factor = 0.2 * math.sqrt(max(M, N))
    back_rows = lax.all_to_all(columns, "tensor", split_axis=0, concat_axis=1, tiled=True)
    scaled = (factor * back_rows.astype(jnp.float32)).astype(jnp.bfloat16)
    every_slot = lax.all_gather(scaled[None], "dp", axis=0, tiled=True)
    matrix_ids = jnp.arange(every_slot.shape[0], dtype=jnp.int32)
    selector = (owner[None, :] == matrix_ids[:, None]).astype(jnp.bfloat16)
    update = jnp.einsum(
        "mg,grn->mrn", selector, every_slot, preferred_element_type=jnp.float32
    ).astype(jnp.bfloat16)
    return (update, new_momentum)


def solution(mesh):
    in_specs = (P("dp", "tensor", None), P("dp", "tensor", None), P())
    out_specs = (P(None, "tensor", None), P("dp", "tensor", None))
    return jax.shard_map(
        per_device, mesh=mesh, in_specs=in_specs, out_specs=out_specs, check_vma=False
    )
```

profile of v0, /device:TPU:0, one launch (start us, length us, event | category | flops | bytes accessed | tf_op | source)
XLA Modules:
  0.0 286.8 jit_solution(11792428714496908145)
XLA Ops:
  7.2 0.0 all-gather.2.cloned.1.call-start
  7.2 2.9 %multiply_reduce_fusion = (f32[]{:T(128)}, f32[1,72,6144]{2,1,0:T(8,128)S(1)}) fusion(bf16[1,72,6144]{2,1,0:T(8,128)(2,1)} %param.3, f32[1,72,6144]{2,1,0:T(8,128)} %param.4), kind=kLoop, calls=%fused_computation.8 | loop fusion | flops 3096575 | bytes 4423684 | tf_op jit(solution)/shard_map/reduce_sum | solution.py:20
  10.1 23.8 %psum.21 = f32[]{:T(128)} all-reduce(f32[]{:T(128)} %get-tuple-element.8), channel_id=1, replica_groups=mesh['dp'=4,'tensor'=8] {'tensor'}, use_global_device_ids=true, to_apply=%region_1.0 | all-reduce | flops 1 | bytes 8 | tf_op jit(solution)/shard_map/psum | solution.py:20
  34.6 0.3 divide_convert_fusion
  34.9 0.2 copy.16
  35.0 0.2 copy.12
  35.2 21.7 %all_to_all.29 = bf16[72,8,768]{2,0,1:T(8,128)(2,1)S(1)} all-to-all(bf16[72,8,768]{2,0,1:T(8,128)(2,1)S(1)} %copy.12), channel_id=1, replica_groups=mesh['dp'=4,'tensor'=8] {'tensor'}, dimensions={1} | all-to-all | bytes 1769472 | tf_op jit(solution)/shard_map/all_to_all | solution.py:22
  56.9 0.9 fusion.17
  57.7 79.9 %all-reduce.2 = bf16[576,576]{1,0:T(8,128)(2,1)S(1)} all-reduce(f32[576,576]{1,0:T(8,128)S(1)} %fusion.17), channel_id=1, replica_groups=mesh['dp'=4,'tensor'=8] {'tensor'}, use_global_device_ids=true, to_apply=%region_2.0 | all-reduce | flops 331776 | bytes 1990656 | tf_op jit(solution)/shard_map/psum | solution.py:24
  137.6 1.6 add_convert_fusion.1
  139.3 0.9 copy-done.3
  140.2 0.9 fusion.18
  141.1 0.0 copy-start.4
  141.1 78.1 %all-reduce.3 = bf16[576,576]{1,0:T(8,128)(2,1)S(1)} all-reduce(f32[576,576]{1,0:T(8,128)S(1)} %fusion.18), channel_id=1, replica_groups=mesh['dp'=4,'tensor'=8] {'tensor'}, use_global_device_ids=true, to_apply=%region_3.0 | all-reduce | flops 331776 | bytes 1990656 | tf_op jit(solution)/shard_map/psum | solution.py:24
  219.2 1.6 add_convert_fusion
  220.8 18.7 %all_to_all.30 = bf16[8,72,768]{2,1,0:T(8,128)(2,1)S(1)} all-to-all(bf16[8,72,768]{2,1,0:T(8,128)(2,1)S(1)} %bitcast.26), channel_id=1, replica_groups=mesh['dp'=4,'tensor'=8] {'tensor'}, dimensions={0} | all-to-all | bytes 1769472 | tf_op jit(solution)/shard_map/all_to_all | solution.py:32
  239.6 0.2 fusion.1
  239.7 0.2 copy.13
  239.9 0.0 copy-start.2
  239.9 1.3 convert_element_type.89
  241.2 0.0 all-gather.2.cloned.1.call-update
  241.2 28.5 %all-gather.2.cloned.1.call-done = bf16[4,72,6144]{2,1,0:T(8,128)(2,1)} async-done(((bf16[1,72,6144]{2,1,0:T(8,128)(2,1)}), bf16[4,72,6144]{2,1,0:T(8,128)(2,1)}) %all-gather.2.cloned.1.call-update) | async-done | bytes 3538960 | tf_op jit(solution)/shard_map/all_gather | solution.py:34
  269.7 6.5 %convolution_convert_fusion = bf16[4,72,6144]{2,0,1:T(4,128)(2,1)S(1)} fusion(bf16[4,72,6144]{2,1,0:T(8,128)(2,1)} %all-gather.2.cloned.1.call-done, s32[4]{0:T(128)S(1)} %copy-done.2), kind=kOutput, calls=%fused_computation | convolution fusion | flops 15925264 | bytes 7077904 | tf_op jit(solution)/shard_map/mg,grn->mrn/dot_general | solution.py:37
  276.2 3.7 %copy.15 = bf16[4,72,6144]{2,1,0:T(8,128)(2,1)} copy(bf16[4,72,6144]{2,0,1:T(4,128)(2,1)S(1)} %convolution_convert_fusion) | data formatting | bytes 7077888
  (7 shorter events, 0.0 us)
Async XLA Ops:
  7.2 27.4 %copy-start.1 = (bf16[1,72,6144]{2,1,0:T(8,128)(2,1)S(1)}, bf16[1,72,6144]{2,1,0:T(8,128)(2,1)}, u32[]{:S(2)}) copy-start(bf16[1,72,6144]{2,1,0:T(8,128)(2,1)} %param.3) | copy-start | bytes 2654212
  7.2 262.5 %all-gather.2.cloned.1.call-start = ((), (), s32[]{:S(2)}) async-start(), calls=%async_computation.2 | async-start | bytes 4423680 | tf_op jit(solution)/shard_map/all_gather | solution.py:34
  10.1 24.7 %copy-start = (f32[1,72,6144]{2,1,0:T(8,128)}, f32[1,72,6144]{2,1,0:T(8,128)S(1)}, u32[]{:S(2)}) copy-start(f32[1,72,6144]{2,1,0:T(8,128)S(1)} %get-tuple-element.9) | copy-start | bytes 5308420
  139.3 0.9 copy-start.3
  141.1 78.1 %copy-start.4 = (bf16[576,768]{1,0:T(8,128)(2,1)S(1)}, bf16[576,768]{1,0:T(8,128)(2,1)}, u32[]{:S(2)}) copy-start(bf16[576,768]{1,0:T(8,128)(2,1)} %copy-done.3) | copy-start | bytes 2654212
  239.9 29.8 %copy-start.2 = (s32[4]{0:T(128)S(1)}, s32[4]{0:T(128)}, u32[]{:S(2)}) copy-start(s32[4]{0:T(128)} %param.5) | copy-start | bytes 52
Sparse Core Ops, SparseCore 0:
  241.3 28.2 all-gather.1
where the time goes:
time: 287 us
  blocking collectives  222 us (77%)
  waiting for transfers between devices  28.5 us (10%)
  between operations  14.8 us (5%)
  matrix products  11.6 us (4%)
  local copies, waits for them, and re-layouts  6.44 us (2%)
  other arithmetic  3.29 us (1%)
    psum x2, blocking collectives, per_device(): lax.psum(jnp.dot(columns, columns.T, preferred_element_type=jnp.float32),...  158 us
    all_gather x1, waiting for transfers between devices, per_device(): every_slot = lax.all_gather(scaled[None], 'dp', axis=0, tiled=True)  28.5 us
    psum x1, blocking collectives, per_device(): total = lax.psum(jnp.sum(direction * direction), 'tensor')  23.8 us
    all_to_all x1, blocking collectives, per_device(): lax.all_to_all(rows_here, 'tensor', split_axis=1, concat_axis=0, tiled=True)  21.7 us
    all_to_all x1, blocking collectives, per_device(): lax.all_to_all(columns, 'tensor', split_axis=0, concat_axis=1, tiled=True)  18.7 us
    dot_general x1, matrix products, per_device(): jnp.einsum('mg,grn->mrn', selector, every_slot, preferred_element_type=jn...  6.52 us
  transfers between devices with their start and end apart: 1, of which 1 were waited for; matrix products, arithmetic and copies ran while one was open for 0% of the time, Pallas kernels for 0%

commit v1 on v0

--- a/solution.py
+++ b/solution.py
@@ -3,6 +3,7 @@
 import jax.numpy as jnp
 from jax import lax
 from jax.sharding import PartitionSpec as P
+from jax.lax import axis_index, axis_size, ppermute
 
 M = 576
 N = 6144
@@ -29,7 +30,24 @@
         applied = jnp.dot(poly, columns, preferred_element_type=jnp.float32)
         columns = (coef_a * columns.astype(jnp.float32) + applied).astype(jnp.bfloat16)
     factor = 0.2 * math.sqrt(max(M, N))
-    back_rows = lax.all_to_all(columns, "tensor", split_axis=0, concat_axis=1, tiled=True)
+    w1, all_values = (axis_size("tensor"), axis_index("tensor"))
+    mid_arr = list(columns.shape)
+    arr_next = columns.shape[0] // w1
+    mid_arr[0] = arr_next
+    state_next = mid_arr[1]
+    mid_arr[1] = state_next * w1
+    back_rows = jnp.zeros(mid_arr, columns.dtype)
+    for tick in range(w1):
+        local_part = lax.dynamic_slice_in_dim(
+            columns, (all_values ^ tick) * arr_next, arr_next, axis=0
+        )
+        if tick:
+            local_part = ppermute(
+                local_part, "tensor", tuple(((idx, idx ^ tick) for idx in range(w1)))
+            )
+        back_rows = lax.dynamic_update_slice_in_dim(
+            back_rows, local_part, (all_values ^ tick) * state_next, axis=1
+        )
     scaled = (factor * back_rows.astype(jnp.float32)).astype(jnp.bfloat16)
     every_slot = lax.all_gather(scaled[None], "dp", axis=0, tiled=True)
     matrix_ids = jnp.arange(every_slot.shape[0], dtype=jnp.int32)

time: 287 us -> 293 us (1.021)
  blocking collectives: 222 us -> 180 us
  waiting for transfers between devices: 28.5 us -> 60.4 us
  starting transfers between devices: 0.04 us -> 14.1 us
    all_to_all x2 -> x0, blocking collectives: 40.4 us -> none  [the longest x1 21.7 us: per_device(): lax.all_to_all(rows_here, 'tensor', split_axis=1, concat_axis=0, tiled=True)]
    all_to_all x0 -> x1, waiting for transfers between devices: none -> 18.8 us  [per_device(): lax.all_to_all(rows_here, 'tensor', split_axis=1, concat_axis=0, tiled=True)]
    ppermute x0 -> x7, waiting for transfers between devices: none -> 10.6 us  [per_device(): ppermute(local_part, 'tensor', tuple(((idx, idx ^ tick) for idx in range(...]
    ppermute x0 -> x7, starting transfers between devices: none -> 10.5 us  [per_device(): ppermute(local_part, 'tensor', tuple(((idx, idx ^ tick) for idx in range(...]
    all_to_all x0 -> x1, starting transfers between devices: none -> 3.55 us  [per_device(): lax.all_to_all(rows_here, 'tensor', split_axis=1, concat_axis=0, tiled=True)]
  transfers between devices with their start and end apart: 1 -> 9, of which waited for: 1 -> 4; matrix products, arithmetic and copies ran while one was open for 0% -> 0% of each run, Pallas kernels for 0% -> 0%
where the time goes in v1:
time: 293 us; the launch traced here: 292 us
  blocking collectives  180 us (61%)
  waiting for transfers between devices  60.4 us (21%)
  between operations  15 us (5%)
  starting transfers between devices  14.1 us (5%)
  matrix products  13.1 us (4%)
  local copies, waits for them, and re-layouts  5.24 us (2%)
  other arithmetic  4.21 us (1%)
    psum x2, blocking collectives, per_device(): lax.psum(jnp.dot(columns, columns.T, preferred_element_type=jnp.float32),...  157 us
    all_gather x1, waiting for transfers between devices, per_device(): every_slot = lax.all_gather(scaled[None], 'dp', axis=0, tiled=True)  31 us
    psum x1, blocking collectives, per_device(): total = lax.psum(jnp.sum(direction * direction), 'tensor')  23.8 us
    all_to_all x1, waiting for transfers between devices, per_device(): lax.all_to_all(rows_here, 'tensor', split_axis=1, concat_axis=0, tiled=True)  18.8 us
    ppermute x7, waiting for transfers between devices, per_device(): ppermute(local_part, 'tensor', tuple(((idx, idx ^ tick) for idx in range(...  10.6 us
    ppermute x7, starting transfers between devices, per_device(): ppermute(local_part, 'tensor', tuple(((idx, idx ^ tick) for idx in range(...  10.5 us
    dot_general x1, matrix products, per_device(): jnp.einsum('mg,grn->mrn', selector, every_slot, preferred_element_type=jn...  6.52 us
  transfers between devices with their start and end apart: 9, of which 4 were waited for; matrix products, arithmetic and copies ran while one was open for 0% of the time, Pallas kernels for 0%

profile of v1, /device:TPU:0, one launch (start us, length us, event | category | flops | bytes accessed | tf_op | source)
XLA Modules:
  0.0 292.4 jit_solution(3061818345895533840)
XLA Ops:
  7.2 2.9 multiply_reduce_fusion
  10.1 23.8 %psum.21 = f32[]{:T(128)} all-reduce(f32[]{:T(128)} %get-tuple-element.6), channel_id=1, replica_groups=mesh['dp'=4,'tensor'=8] {'tensor'}, use_global_device_ids=true, to_apply=%region_1.0 | all-reduce | flops 1 | bytes 8 | tf_op jit(solution)/shard_map/psum | solution.py:21
  34.5 0.3 divide_convert_fusion
  35.0 1.1 copy.7
  36.0 3.6 %all-to-all-start = ((bf16[72,8,768]{2,0,1:T(8,128)(2,1)}), bf16[72,8,768]{2,0,1:T(8,128)(2,1)S(1)}, u32[]{:S(2)}, u32[]{:S(2)}) async-start(bf16[72,8,768]{2,0,1:T(8,128)(2,1)} %copy.7), calls=%async_computation | async-start | bytes 1769472 | tf_op jit(solution)/shard_map/all_to_all | solution.py:23
  39.7 18.8 %all-to-all-done = bf16[72,8,768]{2,0,1:T(8,128)(2,1)S(1)} async-done(((bf16[72,8,768]{2,0,1:T(8,128)(2,1)}), bf16[72,8,768]{2,0,1:T(8,128)(2,1)S(1)}, u32[]{:S(2)}, u32[]{:S(2)}) %all-to-all-start) | async-done | bytes 884768 | tf_op jit(solution)/shard_map/all_to_all | solution.py:23
  58.5 0.9 fusion.16
  59.4 78.3 %all-reduce.2 = bf16[576,576]{1,0:T(8,128)(2,1)S(1)} all-reduce(f32[576,576]{1,0:T(8,128)S(1)} %fusion.16), channel_id=1, replica_groups=mesh['dp'=4,'tensor'=8] {'tensor'}, use_global_device_ids=true, to_apply=%region_2.0 | all-reduce | flops 331776 | bytes 1990656 | tf_op jit(solution)/shard_map/psum | solution.py:25
  137.7 1.6 add_convert_fusion.1
  139.4 0.9 fusion.17
  140.3 78.4 %all-reduce.3 = bf16[576,576]{1,0:T(8,128)(2,1)S(1)} all-reduce(f32[576,576]{1,0:T(8,128)S(1)} %fusion.17), channel_id=1, replica_groups=mesh['dp'=4,'tensor'=8] {'tensor'}, use_global_device_ids=true, to_apply=%region_3.0 | all-reduce | flops 331776 | bytes 1990656 | tf_op jit(solution)/shard_map/psum | solution.py:25
  218.7 3.1 %add_convert_fusion = bf16[576,768]{1,0:T(8,128)(2,1)S(1)} fusion(bf16[576,768]{1,0:T(8,128)(2,1)} %copy-done.3, bf16[576,576]{1,0:T(8,128)(2,1)S(1)} %all-reduce.3), kind=kOutput, calls=%fused_computation.5 | convolution fusion | flops 895242240 | bytes 2433024 | tf_op jit(solution)/shard_map/dot_general | solution.py:30
  222.0 2.2 collective-permute-start
  224.2 2.4 collective-permute-start.6
  226.6 1.0 collective-permute-start.5
  227.6 3.0 %collective-permute-start.4 = (bf16[72,768]{1,0:T(8,128)(2,1)S(1)}, bf16[72,768]{1,0:T(8,128)(2,1)S(1)}, u32[]{:S(2)}, u32[]{:S(2)}) collective-permute-start(bf16[72,768]{1,0:T(8,128)(2,1)S(1)} %get-tuple-element.10), channel_id=1, source_target_pairs={{0,5},{1,4},{2,7},{3,6},{4,1},{5,0},{6,3},{7,2},{8,13},{9,12},{10,... | collective-permute-start | bytes 331784 | tf_op jit(solution)/shard_map/ppermute | solution.py:45
  230.6 1.2 collective-permute-start.3
  231.8 0.7 collective-permute-start.1
  232.5 5.0 %collective-permute-done.1 = bf16[72,768]{1,0:T(8,128)(2,1)S(1)} collective-permute-done((bf16[72,768]{1,0:T(8,128)(2,1)S(1)}, bf16[72,768]{1,0:T(8,128)(2,1)S(1)}, u32[]{:S(2)}, u32[]{:S(2)}) %collective-permute-start.1) | collective-permute-done | bytes 110624 | tf_op jit(solution)/shard_map/ppermute | solution.py:45
  237.5 5.6 %collective-permute-done.2 = bf16[72,768]{1,0:T(8,128)(2,1)S(1)} collective-permute-done((bf16[72,768]{1,0:T(8,128)(2,1)S(1)}, bf16[72,768]{1,0:T(8,128)(2,1)S(1)}, u32[]{:S(2)}, u32[]{:S(2)}) %collective-permute-start.2) | collective-permute-done | bytes 110624 | tf_op jit(solution)/shard_map/ppermute | solution.py:45
  243.3 1.1 multiply_convert_fusion
  244.4 31.0 %all-gather.3.cloned.1.call-done = bf16[288,6144]{1,0:T(8,128)(2,1)} async-done(((bf16[72,6144]{1,0:T(8,128)(2,1)}), bf16[288,6144]{1,0:T(8,128)(2,1)}) %all-gather.3.cloned.1.call-update) | async-done | bytes 3538960 | tf_op jit(solution)/shard_map/all_gather | solution.py:52
  275.3 6.5 %convolution_convert_fusion = bf16[4,72,6144]{2,0,1:T(4,128)(2,1)S(1)} fusion(bf16[4,72,6144]{2,1,0:T(8,128)(2,1)} %bitcast.24, s32[4]{0:T(128)S(1)} %copy-done.2), kind=kOutput, calls=%fused_computation | convolution fusion | flops 15925264 | bytes 7077904 | tf_op jit(solution)/shard_map/mg,grn->mrn/dot_general | solution.py:55
  281.9 3.7 %copy.9 = bf16[4,72,6144]{2,1,0:T(8,128)(2,1)} copy(bf16[4,72,6144]{2,0,1:T(4,128)(2,1)S(1)} %convolution_convert_fusion) | data formatting | bytes 7077888
  (26 shorter events, 0.5 us)
Async XLA Ops:
  7.2 27.4 %copy-start.1 = (bf16[1,72,6144]{2,1,0:T(8,128)(2,1)S(1)}, bf16[1,72,6144]{2,1,0:T(8,128)(2,1)}, u32[]{:S(2)}) copy-start(bf16[1,72,6144]{2,1,0:T(8,128)(2,1)} %param.3) | copy-start | bytes 2654212
  10.1 24.7 %copy-start = (f32[1,72,6144]{2,1,0:T(8,128)}, f32[1,72,6144]{2,1,0:T(8,128)S(1)}, u32[]{:S(2)}) copy-start(f32[1,72,6144]{2,1,0:T(8,128)S(1)} %get-tuple-element.7) | copy-start | bytes 5308420
  36.0 22.5 %all-to-all-start = ((bf16[72,8,768]{2,0,1:T(8,128)(2,1)}), bf16[72,8,768]{2,0,1:T(8,128)(2,1)S(1)}, u32[]{:S(2)}, u32[]{:S(2)}) async-start(bf16[72,8,768]{2,0,1:T(8,128)(2,1)} %copy.7), calls=%async_computation | async-start | bytes 1769472 | tf_op jit(solution)/shard_map/all_to_all | solution.py:23
  39.6 235.7 %all-gather.3.cloned.1.call-start = ((), (), s32[]{:S(2)}) async-start(), calls=%async_computation.1 | async-start | bytes 4423680 | tf_op jit(solution)/shard_map/all_gather | solution.py:52
  139.3 0.9 copy-start.3
  222.0 9.8 %collective-permute-start = (bf16[72,768]{1,0:T(8,128)(2,1)S(1)}, bf16[72,768]{1,0:T(8,128)(2,1)S(1)}, u32[]{:S(2)}, u32[]{:S(2)}) collective-permute-start(bf16[72,768]{1,0:T(8,128)(2,1)S(1)} %get-tuple-element.14), channel_id=1, source_target_pairs={{0,1},{1,0},{2,3},{3,2},{4,5},{5,4},{6,7},{7,6},{8,9},{9,8},{10,11... | collective-permute-start | bytes 331784 | tf_op jit(solution)/shard_map/ppermute | solution.py:45
  224.2 19.1 %collective-permute-start.6 = (bf16[72,768]{1,0:T(8,128)(2,1)S(1)}, bf16[72,768]{1,0:T(8,128)(2,1)S(1)}, u32[]{:S(2)}, u32[]{:S(2)}) collective-permute-start(bf16[72,768]{1,0:T(8,128)(2,1)S(1)} %get-tuple-element.8), channel_id=1, source_target_pairs={{0,7},{1,6},{2,5},{3,4},{4,3},{5,2},{6,1},{7,0},{8,15},{9,14},{10,... | collective-permute-start | bytes 331784 | tf_op jit(solution)/shard_map/ppermute | solution.py:45
  226.6 16.7 %collective-permute-start.5 = (bf16[72,768]{1,0:T(8,128)(2,1)S(1)}, bf16[72,768]{1,0:T(8,128)(2,1)S(1)}, u32[]{:S(2)}, u32[]{:S(2)}) collective-permute-start(bf16[72,768]{1,0:T(8,128)(2,1)S(1)} %get-tuple-element.9), channel_id=1, source_target_pairs={{0,6},{1,7},{2,4},{3,5},{4,2},{5,3},{6,0},{7,1},{8,14},{9,15},{10,... | collective-permute-start | bytes 331784 | tf_op jit(solution)/shard_map/ppermute | solution.py:45
  227.6 15.6 %collective-permute-start.4 = (bf16[72,768]{1,0:T(8,128)(2,1)S(1)}, bf16[72,768]{1,0:T(8,128)(2,1)S(1)}, u32[]{:S(2)}, u32[]{:S(2)}) collective-permute-start(bf16[72,768]{1,0:T(8,128)(2,1)S(1)} %get-tuple-element.10), channel_id=1, source_target_pairs={{0,5},{1,4},{2,7},{3,6},{4,1},{5,0},{6,3},{7,2},{8,13},{9,12},{10,... | collective-permute-start | bytes 331784 | tf_op jit(solution)/shard_map/ppermute | solution.py:45
  230.6 12.6 %collective-permute-start.3 = (bf16[72,768]{1,0:T(8,128)(2,1)S(1)}, bf16[72,768]{1,0:T(8,128)(2,1)S(1)}, u32[]{:S(2)}, u32[]{:S(2)}) collective-permute-start(bf16[72,768]{1,0:T(8,128)(2,1)S(1)} %get-tuple-element.11), channel_id=1, source_target_pairs={{0,4},{1,5},{2,6},{3,7},{4,0},{5,1},{6,2},{7,3},{8,12},{9,13},{10,... | collective-permute-start | bytes 331784 | tf_op jit(solution)/shard_map/ppermute | solution.py:45
  231.8 5.7 %collective-permute-start.1 = (bf16[72,768]{1,0:T(8,128)(2,1)S(1)}, bf16[72,768]{1,0:T(8,128)(2,1)S(1)}, u32[]{:S(2)}, u32[]{:S(2)}) collective-permute-start(bf16[72,768]{1,0:T(8,128)(2,1)S(1)} %get-tuple-element.13), channel_id=1, source_target_pairs={{0,2},{1,3},{2,0},{3,1},{4,6},{5,7},{6,4},{7,5},{8,10},{9,11},{10,... | collective-permute-start | bytes 331784 | tf_op jit(solution)/shard_map/ppermute | solution.py:45
  237.5 5.6 %collective-permute-start.2 = (bf16[72,768]{1,0:T(8,128)(2,1)S(1)}, bf16[72,768]{1,0:T(8,128)(2,1)S(1)}, u32[]{:S(2)}, u32[]{:S(2)}) collective-permute-start(bf16[72,768]{1,0:T(8,128)(2,1)S(1)} %get-tuple-element.12), channel_id=1, source_target_pairs={{0,3},{1,2},{2,1},{3,0},{4,7},{5,6},{6,5},{7,4},{8,11},{9,10},{10,... | collective-permute-start | bytes 331784 | tf_op jit(solution)/shard_map/ppermute | solution.py:45
  243.1 32.2 %copy-start.2 = (s32[4]{0:T(128)S(1)}, s32[4]{0:T(128)}, u32[]{:S(2)}) copy-start(s32[4]{0:T(128)} %param.5) | copy-start | bytes 52
Sparse Core Ops, SparseCore 0:
  244.5 30.7 all-gather.2
